TPU v7x, 128 devices: a whole 4x4x4 slice. The times are simulated.
128 devices in a mesh: row: 16 (over x, z), col: 8 (over y, core).
Axes of the slice: x: 4, y: 4, z: 4, core: 2. Of those that a mesh axis runs over, the one named last changes fastest.
Arguments:
- a_vals: float32 [16, 8, 448, 4096], P('row', 'col'), may hold values from -0.1875 to 0.1875
- a_row: int32 [16, 8, 448], P('row', 'col'), may hold values from 0 to 63
- a_col: int32 [16, 8, 448], P('row', 'col'), may hold values from 0 to 127
- a_slot: int32 [16, 8, 3, 448], P('row', 'col'), may hold values from 0 to 5
- a_count: int32 [16, 8], P('row', 'col'), may hold values from 1 to 448, as said below
- p_vals: float32 [1024, 3, 4096], P(('row', 'col')), may hold values from -0.75 to 0.75
- p_owner: int32 [1024, 3], P(('row', 'col')), may hold values from 0 to 15, all different within a row; in each aligned block of 8 rows (0 to 7, 8 to 15, ...) at most 2 rows name the same one
- p_sub: int32 [1024, 3], P(('row', 'col')), may hold values from 0 to 7
- ap_cslot: int32 [1024, 3, 6], P(('row', 'col')), may hold values from 0 to 26
Outputs:
- coarse: float32 [128, 27, 4096], P(('row', 'col'))
Inputs may be any that keep to these rules, and one draw needn't show every extreme that they name: `a_count`: at least one device holds exactly 448 listed blocks. `p_owner`: the 3 entries of a fine block row differ; among the rows of one device each row group is named at most 2 times.
All inputs are finite; a program needn't handle non-finite values.
Results may differ from a plain program's by a relative error of at most 0.0001.
Values sent between devices are 32-bit elements; how exact they have to be, the bound alone decides.
No kernel may reach another device: no remote copies, remote signals or barrier semaphores. Data moves between devices by JAX's collectives and lax.ppermute only.
A program may use at most 128 MiB of HBM per device.

v0:
```python
import jax
import jax.numpy as jnp
from jax import lax
from jax.sharding import PartitionSpec as P

BLOCK = 64
CPD = 1
TAP = 6
TC = 27
highest = lax.Precision.HIGHEST
tile_batch = 16


def on_device(a_vals, a_row, a_col, a_slot, a_count, p_vals, p_owner, p_sub, ap_cslot):
    row_devices = lax.axis_size("row")
    col_devices = lax.axis_size("col")
    capacity = a_vals.shape[2]
    rows_dev = p_vals.shape[0]
    branches = p_vals.shape[1]
    tile_len = p_vals.shape[2]
    group_rows = rows_dev * col_devices
    group_coarse = CPD * col_devices
    per_peer = max(2, 3 * rows_dev * branches // (2 * row_devices))
    matrix_tiles = a_vals.reshape(capacity, BLOCK, BLOCK)
    tile_rows = a_row.reshape(capacity)
    tile_cols = a_col.reshape(capacity)
    tile_slots = a_slot.reshape(branches, capacity)
    tile_count = a_count.reshape(())
    panel = lax.all_gather(p_vals, "row", axis=0, tiled=True)
    panel_tiles = panel.reshape(rows_dev * row_devices, branches, BLOCK, BLOCK)

    def add_batch(batch_index, partial_value):
        first_tile = batch_index * tile_batch
        block_tiles = lax.dynamic_slice_in_dim(matrix_tiles, first_tile, tile_batch, 0)
        block_rows = lax.dynamic_slice_in_dim(tile_rows, first_tile, tile_batch, 0)
        block_cols = lax.dynamic_slice_in_dim(tile_cols, first_tile, tile_batch, 0)
        block_slots = lax.dynamic_slice_in_dim(tile_slots, first_tile, tile_batch, 1)
        right_tiles = jnp.take(panel_tiles, block_cols, axis=0)
        products = jnp.einsum("tij,tsjk->tsik", block_tiles, right_tiles, precision=highest)
        is_live = first_tile + jnp.arange(tile_batch, dtype=jnp.int32) < tile_count
        products = jnp.where(is_live[:, None, None, None], products, 0.0)
        target = block_rows[:, None] * TAP + block_slots.T
        return partial_value.at[target.reshape(-1)].add(
            products.reshape(tile_batch * branches, tile_len)
        )

    batches = (tile_count + tile_batch - 1) // tile_batch
    partial_value = lax.fori_loop(
        0, batches, add_batch, jnp.zeros((group_rows * TAP, tile_len), jnp.float32)
    )
    ap_rows = lax.psum_scatter(
        partial_value.reshape(group_rows, TAP, tile_len), "col", scatter_dimension=0, tiled=True
    )
    item_count = rows_dev * branches
    owners = p_owner.reshape(item_count)
    serial = jnp.arange(item_count, dtype=jnp.int32)
    earlier = (owners[:, None] == owners[None, :]) & (serial[None, :] < serial[:, None])
    placed = owners * per_peer + jnp.sum(earlier.astype(jnp.int32), axis=1)
    slots_total = row_devices * per_peer
    metadata = jnp.concatenate(
        [p_sub.reshape(item_count, 1), ap_cslot.reshape(item_count, TAP)], axis=1
    ).astype(jnp.float32)
    meta_send = jnp.zeros((slots_total, TAP + 1), jnp.float32).at[placed].set(metadata)
    ap_items = jnp.broadcast_to(ap_rows[:, None], (rows_dev, branches, TAP, tile_len)).reshape(
        item_count, TAP, tile_len
    )
    packed = jnp.concatenate([p_vals.reshape(item_count, 1, tile_len), ap_items], axis=1)
    outgoing = jnp.zeros((slots_total, TAP + 1, tile_len), jnp.float32).at[placed].set(packed)
    incoming, meta_in = (
        lax.all_to_all(outgoing, "row", split_axis=0, concat_axis=0, tiled=True),
        lax.all_to_all(meta_send, "row", split_axis=0, concat_axis=0, tiled=True),
    )
    left_in = incoming[:, 0].reshape(slots_total, BLOCK, BLOCK)
    right_in = incoming[:, 1:].reshape(slots_total, TAP, BLOCK, BLOCK)
    arrived = jnp.einsum("ejk,eqjl->eqkl", left_in, right_in, precision=highest).reshape(
        slots_total, TAP, tile_len
    )
    arrived_index = meta_in.astype(jnp.int32)
    target = arrived_index[:, :1] * TC + arrived_index[:, 1:]
    coarse_part = (
        jnp.zeros((group_coarse * TC, tile_len), jnp.float32)
        .at[target.reshape(-1)]
        .add(arrived.reshape(slots_total * TAP, tile_len))
    )
    coarse = lax.psum_scatter(
        coarse_part.reshape(group_coarse, TC, tile_len), "col", scatter_dimension=0, tiled=True
    )
    return coarse


def solution(mesh):
    placed = (
        P("row", "col", None, None),
        P("row", "col", None),
        P("row", "col", None),
        P("row", "col", None, None),
        P("row", "col"),
        P(("row", "col"), None, None),
        P(("row", "col"), None),
        P(("row", "col"), None),
        P(("row", "col"), None, None),
    )
    return jax.shard_map(
        on_device,
        mesh=mesh,
        in_specs=placed,
        out_specs=P(("row", "col"), None, None),
        check_vma=False,
    )
```

profile of v0, /device:TPU:0, one launch (start us, length us, event | category | flops | bytes accessed | tf_op | source)
XLA Modules:
  0.0 882.7 jit_solution(11410659418948693144)
XLA Ops:
  8.0 9.0 %copy.84 = f32[1,1,448,4096]{2,3,1,0:T(8,128)} copy(f32[1,1,448,4096]{3,2,1,0:T(8,128)} %param.11) | data formatting | bytes 14680064 | tf_op args[0]
  17.0 11.9 %copy.86 = f32[448,64,64]{2,1,0:T(8,128)} copy(f32[448,64,64]{0,2,1:T(8,128)} %bitcast.49) | data formatting | bytes 14680064 | tf_op jit(solution)/shard_map/while | solution.py:48
  29.0 44.5 %all-gather.2.cloned.1.call-done = f32[128,3,4096]{2,0,1:T(8,128)} async-done(((f32[8,3,4096]{2,0,1:T(8,128)}), f32[128,3,4096]{2,0,1:T(8,128)}) %all-gather.2.cloned.1.call-update) | async-done | bytes 6291472 | tf_op jit(solution)/shard_map/all_gather | solution.py:29
  73.5 6.6 copy.83
  80.1 12.7 %copy.85 = f32[128,3,64,64]{3,2,1,0:T(8,128)} copy(f32[128,3,64,64]{0,3,2,1:T(8,128)} %bitcast.50) | data formatting | bytes 12582912 | tf_op jit(solution)/shard_map/while | solution.py:48
  92.8 3.3 broadcast_in_dim.53
  96.2 38.7 %while.10 = (s32[]{:T(128)}, f32[384,4096]{1,0:T(8,128)}, s32[]{:T(128)}, s32[448]{0:T(512)}, s32[3,448]{0,1:T(8,128)S(1)}, /*index=5*/s32[]{:T(128)}, s32[448]{...) while((s32[]{:T(128)}, f32[384,4096]{1,0:T(8,128)}, ...), condition=%wide.region_4.5_spmd, body=%wide.region_2.4_spmd.sunk | while | flops 151586128 | bytes 9181187 | solution.py:48
  97.6 5.2 gather_fusion
  102.8 3.9 select_bitcast_fusion.2
  108.6 6.9 scatter_fusion
  116.9 5.2 gather_fusion
  122.2 3.9 select_bitcast_fusion.2
  128.0 6.9 scatter_fusion
  134.9 7.5 reshape.161
  145.3 508.0 %all-to-all-start = ((f32[16,2,7]{2,1,0:T(2,128)}), f32[16,2,7]{2,1,0:T(2,128)S(1)}, u32[]{:S(2)}, u32[]{:S(2)}) async-start(f32[16,2,7]{2,1,0:T(2,128)} %bitcast.7), calls=%async_computation | async-start | bytes 32768 | tf_op jit(solution)/shard_map/all_to_all | solution.py:71
  653.8 43.9 %reduce-scatter.3.cloned.1.call-done = f32[8,6,4096]{2,1,0:T(8,128)} async-done(((f32[64,6,4096]{2,1,0:T(8,128)}), f32[8,6,4096]{2,1,0:T(8,128)}) %reduce-scatter.3.cloned.1.call-update) | async-done | bytes 786448 | tf_op jit(solution)/shard_map/reduce_scatter | solution.py:51
  700.2 2.6 reshape.162
  702.8 1.8 pad_maximum_fusion
  706.2 2.4 broadcast_in_dim.52
  708.7 6.6 scatter_fusion.1
  715.3 7.0 all-to-all-start.1
  722.6 56.7 %all-to-all-done.1 = f32[32,7,4096]{2,1,0:T(8,128)} async-done(((f32[32,7,4096]{2,1,0:T(8,128)}), f32[32,7,4096]{2,1,0:T(8,128)}, u32[]{:S(2)}, u32[]{:S(2)}) %all-to-all-start.1) | async-done | bytes 3670048 | tf_op jit(solution)/shard_map/all_to_all | solution.py:70
  779.3 5.1 slice.20
  784.4 6.8 reshape.208
  791.3 3.6 slice_reduce_fusion
  795.2 13.3 %convolution_bitcast_fusion = f32[32,6,64,64]{2,3,1,0:T(8,128)} fusion(f32[32,6,64,64]{3,2,1,0:T(8,128)} %reshape.208, f32[32,64,64,1]{2,1,0,3:T(8,128)S(1)} %reshape.207), kind=kOutput, calls=%fused_computation.23 | convolution fusion | flops 603979776 | bytes 6815744 | tf_op jit(solution)/shard_map/ejk,eqjl->eqkl/dot_general | solution.py:75
  808.5 6.6 copy.91
  815.1 5.9 reshape.201
  821.0 6.7 scatter_custom_fusion.3
  827.8 2.4 reshape.164
  830.2 43.8 %reduce-scatter.5.cloned.1.call-done = f32[1,27,4096]{2,1,0:T(8,128)} async-done(((f32[8,27,4096]{2,1,0:T(8,128)}), f32[1,27,4096]{2,1,0:T(8,128)}) %reduce-scatter.5.cloned.1.call-update) | async-done | bytes 442384 | tf_op jit(solution)/shard_map/reduce_scatter | solution.py:85
  874.0 2.3 copy.92
  (63 shorter events, 15.8 us)
Async XLA Ops:
  6.5 66.9 %all-gather.2.cloned.1.call-start = ((), (), s32[]{:S(2)}) async-start(), calls=%async_computation.4 | async-start | bytes 6684672 | tf_op jit(solution)/shard_map/all_gather | solution.py:29
  7.3 690.4 %reduce-scatter.3.cloned.1.call-start = ((), (), s32[]{:S(2)}) async-start(), calls=%async_computation.5 | async-start | bytes 9437184 | tf_op jit(solution)/shard_map/reduce_scatter | solution.py:51
  17.0 11.9 %copy-start.3 = (s32[1,1,3,448]{3,1,2,0:T(1,128)S(1)}, s32[1,1,3,448]{3,1,2,0:T(1,128)}, u32[]{:S(2)}) copy-start(s32[1,1,3,448]{3,1,2,0:T(1,128)} %param.14) | copy-start | bytes 16132
  142.4 0.7 copy-start.2
  142.4 1.0 copy-start.1
  142.4 1.2 copy-start.4
  142.4 510.9 %copy-start = (f32[8,3,4096]{2,0,1:T(8,128)S(1)}, f32[8,3,4096]{2,0,1:T(8,128)}, u32[]{:S(2)}) copy-start(f32[8,3,4096]{2,0,1:T(8,128)} %param.16) | copy-start | bytes 1179652
  144.1 1.2 copy-start.5
  145.3 570.0 %all-to-all-start = ((f32[16,2,7]{2,1,0:T(2,128)}), f32[16,2,7]{2,1,0:T(2,128)S(1)}, u32[]{:S(2)}, u32[]{:S(2)}) async-start(f32[16,2,7]{2,1,0:T(2,128)} %bitcast.7), calls=%async_computation | async-start | bytes 32768 | tf_op jit(solution)/shard_map/all_to_all | solution.py:71
  706.2 2.4 copy-start.6
  715.3 64.1 %all-to-all-start.1 = ((f32[32,7,4096]{2,1,0:T(8,128)}), f32[32,7,4096]{2,1,0:T(8,128)}, u32[]{:S(2)}, u32[]{:S(2)}) async-start(f32[32,7,4096]{2,1,0:T(8,128)} %scatter_fusion.1), calls=%async_computation.2 | async-start | bytes 8388608 | tf_op jit(solution)/shard_map/all_to_all | solution.py:70
  722.3 151.7 %reduce-scatter.5.cloned.1.call-start = ((), (), s32[]{:S(2)}) async-start(), calls=%async_computation.6 | async-start | bytes 4718592 | tf_op jit(solution)/shard_map/reduce_scatter | solution.py:85
Sparse Core Ops, SparseCore 0:
  9.5 63.8 all-gather.1
  142.6 555.0 reduce-scatter.2
  830.3 43.5 reduce-scatter.4
where the time goes:
time: 889 us; the launch traced here: 883 us
  starting transfers between devices  515 us (58%)
  waiting for transfers between devices  190 us (21%)
  local copies, waits for them, and re-layouts  116 us (13%)
  other arithmetic  27.3 us (3%)
  matrix products  21 us (2%)
  between operations  14 us (2%)
    all_to_all x1, starting transfers between devices, on_device(): lax.all_to_all(meta_send, 'row', split_axis=0, concat_axis=0, tiled=True)  508 us
    all_to_all x1, waiting for transfers between devices, on_device(): lax.all_to_all(outgoing, 'row', split_axis=0, concat_axis=0, tiled=True)  56.7 us
    all_gather x1, waiting for transfers between devices, on_device(): panel = lax.all_gather(p_vals, 'row', axis=0, tiled=True)  44.5 us
    reduce_scatter x1, waiting for transfers between devices, on_device(): lax.psum_scatter(partial_value.reshape(group_rows, TAP, tile_len), 'col',...  43.9 us
    reduce_scatter x1, waiting for transfers between devices, on_device(): lax.psum_scatter(coarse_part.reshape(group_coarse, TC, tile_len), 'col',...  43.8 us
    while x2, local copies, waits for them, and re-layouts, on_device(): lax.fori_loop(0, batches, add_batch, jnp.zeros((group_rows * TAP, tile_le...  24.6 us
  transfers between devices with their start and end apart: 5, of which 4 were waited for; matrix products, arithmetic and copies ran while one was open for 5% of the time, Pallas kernels for 0%

commit v1 on v0

--- a/solution.py
+++ b/solution.py
@@ -26,7 +26,11 @@
     tile_cols = a_col.reshape(capacity)
     tile_slots = a_slot.reshape(branches, capacity)
     tile_count = a_count.reshape(())
-    panel = lax.all_gather(p_vals, "row", axis=0, tiled=True)
+    count = lax.axis_size("row")
+    repeats = [count if d == 0 else 1 for d in range(p_vals.ndim)]
+    panel = lax.all_to_all(
+        jnp.tile(p_vals, repeats), "row", split_axis=0, concat_axis=0, tiled=True
+    )
     panel_tiles = panel.reshape(rows_dev * row_devices, branches, BLOCK, BLOCK)
 
     def add_batch(batch_index, partial_value):

time: 889 us -> 995 us (1.12)
  waiting for transfers between devices: 190 us -> 270 us
  local copies, waits for them, and re-layouts: 116 us -> 128 us
  starting transfers between devices: 515 us -> 527 us
    all_to_all x0 -> x1, waiting for transfers between devices: none -> 126 us  [on_device(): lax.all_to_all(jnp.tile(p_vals, repeats), 'row', split_axis=0, concat_axi...]
    all_gather x1 -> x0, waiting for transfers between devices: 44.5 us -> none  [on_device(): panel = lax.all_gather(p_vals, 'row', axis=0, tiled=True)]
  transfers between devices with their start and end apart: 5 -> 5, of which waited for: 4 -> 4; matrix products, arithmetic and copies ran while one was open for 5% -> 4% of each run, Pallas kernels for 0% -> 0%
where the time goes in v1:
time: 995 us; the launch traced here: 988 us
  starting transfers between devices  527 us (53%)
  waiting for transfers between devices  270 us (27%)
  local copies, waits for them, and re-layouts  128 us (13%)
  other arithmetic  27.3 us (3%)
  matrix products  21 us (2%)
  between operations  14.3 us (1%)
    all_to_all x1, starting transfers between devices, on_device(): lax.all_to_all(meta_send, 'row', split_axis=0, concat_axis=0, tiled=True)  512 us
    all_to_all x1, waiting for transfers between devices, on_device(): lax.all_to_all(jnp.tile(p_vals, repeats), 'row', split_axis=0, concat_axi...  126 us
    all_to_all x1, waiting for transfers between devices, on_device(): lax.all_to_all(outgoing, 'row', split_axis=0, concat_axis=0, tiled=True)  56.7 us
    reduce_scatter x1, waiting for transfers between devices, on_device(): lax.psum_scatter(coarse_part.reshape(group_coarse, TC, tile_len), 'col',...  44 us
    reduce_scatter x1, waiting for transfers between devices, on_device(): lax.psum_scatter(partial_value.reshape(group_rows, TAP, tile_len), 'col',...  43.8 us
    while x2, local copies, waits for them, and re-layouts, on_device(): lax.fori_loop(0, batches, add_batch, jnp.zeros((group_rows * TAP, tile_le...  24.6 us
  transfers between devices with their start and end apart: 5, of which 4 were waited for; matrix products, arithmetic and copies ran while one was open for 4% of the time, Pallas kernels for 0%

profile of v1, /device:TPU:0, one launch (start us, length us, event | category | flops | bytes accessed | tf_op | source)
XLA Modules:
  0.0 988.1 jit_solution(5635718491444892311)
XLA Ops:
  8.3 7.7 copy.84
  15.9 8.0 all-to-all-start.1
  24.7 9.0 copy.86
  33.7 11.8 %copy.88 = f32[448,64,64]{2,1,0:T(8,128)} copy(f32[448,64,64]{0,2,1:T(8,128)} %bitcast.51) | data formatting | bytes 14680064 | tf_op jit(solution)/shard_map/while | solution.py:52
  45.7 125.9 %all-to-all-done.1 = f32[128,3,4096]{2,1,0:T(4,128)} async-done(((f32[128,3,4096]{2,1,0:T(4,128)}), f32[128,3,4096]{2,1,0:T(4,128)}, u32[]{:S(2)}, u32[]{:S(2)}) %all-to-all-start.1) | async-done | bytes 6291488 | tf_op jit(solution)/shard_map/all_to_all | solution.py:31
  171.5 9.1 copy.85
  180.6 12.7 %copy.87 = f32[128,3,64,64]{3,2,1,0:T(8,128)} copy(f32[128,3,64,64]{0,3,2,1:T(8,128)} %bitcast.52) | data formatting | bytes 12582912 | tf_op jit(solution)/shard_map/while | solution.py:52
  193.4 3.3 broadcast_in_dim.53
  196.7 38.7 %while.10 = (s32[]{:T(128)}, f32[384,4096]{1,0:T(8,128)}, s32[]{:T(128)}, s32[448]{0:T(512)}, s32[3,448]{0,1:T(8,128)S(1)}, /*index=5*/s32[]{:T(128)}, s32[448]{...) while((s32[]{:T(128)}, f32[384,4096]{1,0:T(8,128)}, ...), condition=%wide.region_4.5_spmd, body=%wide.region_2.4_spmd.sunk | while | flops 151586128 | bytes 9181187 | solution.py:52
  198.1 5.2 gather_fusion
  203.4 3.9 select_bitcast_fusion.2
  209.2 6.9 scatter_fusion
  217.5 5.2 gather_fusion
  222.7 3.9 select_bitcast_fusion.2
  228.5 6.9 scatter_fusion
  235.4 7.5 reshape.165
  245.9 512.3 %all-to-all-start = ((f32[16,2,7]{2,1,0:T(2,128)}), f32[16,2,7]{2,1,0:T(2,128)S(1)}, u32[]{:S(2)}, u32[]{:S(2)}) async-start(f32[16,2,7]{2,1,0:T(2,128)} %bitcast.7), calls=%async_computation | async-start | bytes 32768 | tf_op jit(solution)/shard_map/all_to_all | solution.py:75
  758.7 43.8 %reduce-scatter.3.cloned.1.call-done = f32[8,6,4096]{2,1,0:T(8,128)} async-done(((f32[64,6,4096]{2,1,0:T(8,128)}), f32[8,6,4096]{2,1,0:T(8,128)}) %reduce-scatter.3.cloned.1.call-update) | async-done | bytes 786448 | tf_op jit(solution)/shard_map/reduce_scatter | solution.py:55
  805.0 2.6 reshape.166
  811.1 2.4 broadcast_in_dim.52
  813.5 6.6 scatter_fusion.1
  820.1 7.0 all-to-all-start.2
  827.5 56.7 %all-to-all-done.2 = f32[32,7,4096]{2,1,0:T(8,128)} async-done(((f32[32,7,4096]{2,1,0:T(8,128)}), f32[32,7,4096]{2,1,0:T(8,128)}, u32[]{:S(2)}, u32[]{:S(2)}) %all-to-all-start.2) | async-done | bytes 3670048 | tf_op jit(solution)/shard_map/all_to_all | solution.py:74
  884.2 5.1 slice.20
  889.3 6.8 reshape.212
  896.1 3.6 slice_reduce_fusion
  900.1 13.3 %convolution_bitcast_fusion = f32[32,6,64,64]{2,3,1,0:T(8,128)} fusion(f32[32,6,64,64]{3,2,1,0:T(8,128)} %reshape.212, f32[32,64,64,1]{2,1,0,3:T(8,128)S(1)} %reshape.211), kind=kOutput, calls=%fused_computation.24 | convolution fusion | flops 603979776 | bytes 6815744 | tf_op jit(solution)/shard_map/ejk,eqjl->eqkl/dot_general | solution.py:79
  913.3 6.6 copy.93
  919.9 5.9 reshape.205
  925.8 6.7 scatter_custom_fusion.3
  932.6 2.4 reshape.168
  935.0 44.0 %reduce-scatter.5.cloned.1.call-done = f32[1,27,4096]{2,1,0:T(8,128)} async-done(((f32[8,27,4096]{2,1,0:T(8,128)}), f32[1,27,4096]{2,1,0:T(8,128)}) %reduce-scatter.5.cloned.1.call-update) | async-done | bytes 442384 | tf_op jit(solution)/shard_map/reduce_scatter | solution.py:89
  (64 shorter events, 20.9 us)
Async XLA Ops:
  15.9 155.6 %all-to-all-start.1 = ((f32[128,3,4096]{2,1,0:T(4,128)}), f32[128,3,4096]{2,1,0:T(4,128)}, u32[]{:S(2)}, u32[]{:S(2)}) async-start(f32[128,3,4096]{2,1,0:T(4,128)} %copy.84), calls=%async_computation.1 | async-start | bytes 16777216 | tf_op jit(solution)/shard_map/all_to_all | solution.py:31
  24.0 778.5 %reduce-scatter.3.cloned.1.call-start = ((), (), s32[]{:S(2)}) async-start(), calls=%async_computation.5 | async-start | bytes 9437184 | tf_op jit(solution)/shard_map/reduce_scatter | solution.py:55
  33.7 11.8 %copy-start.3 = (s32[1,1,3,448]{3,1,2,0:T(1,128)S(1)}, s32[1,1,3,448]{3,1,2,0:T(1,128)}, u32[]{:S(2)}) copy-start(s32[1,1,3,448]{3,1,2,0:T(1,128)} %param.14) | copy-start | bytes 16132
  243.0 0.7 copy-start.2
  243.0 1.0 copy-start.1
  243.0 1.2 copy-start.4
  243.0 515.3 %copy-start = (f32[8,3,4096]{2,0,1:T(8,128)S(1)}, f32[8,3,4096]{2,0,1:T(8,128)}, u32[]{:S(2)}) copy-start(f32[8,3,4096]{2,0,1:T(8,128)} %param.16) | copy-start | bytes 1179652
  244.6 1.2 copy-start.5
  245.9 574.2 %all-to-all-start = ((f32[16,2,7]{2,1,0:T(2,128)}), f32[16,2,7]{2,1,0:T(2,128)S(1)}, u32[]{:S(2)}, u32[]{:S(2)}) async-start(f32[16,2,7]{2,1,0:T(2,128)} %bitcast.7), calls=%async_computation | async-start | bytes 32768 | tf_op jit(solution)/shard_map/all_to_all | solution.py:75
  811.0 2.4 copy-start.6
  820.1 64.1 %all-to-all-start.2 = ((f32[32,7,4096]{2,1,0:T(8,128)}), f32[32,7,4096]{2,1,0:T(8,128)}, u32[]{:S(2)}, u32[]{:S(2)}) async-start(f32[32,7,4096]{2,1,0:T(8,128)} %scatter_fusion.1), calls=%async_computation.3 | async-start | bytes 8388608 | tf_op jit(solution)/shard_map/all_to_all | solution.py:74
  827.1 151.9 %reduce-scatter.5.cloned.1.call-start = ((), (), s32[]{:S(2)}) async-start(), calls=%async_computation.6 | async-start | bytes 4718592 | tf_op jit(solution)/shard_map/reduce_scatter | solution.py:89
Sparse Core Ops, SparseCore 0:
  243.1 559.3 reduce-scatter.2
  935.1 43.8 reduce-scatter.4
